TPU v7x, 256 devices: a whole 4x4x8 slice. The times are simulated.
256 devices in a mesh: tm: 128 (over z, y_lo, x, core), net: 2 (over y_hi).
Axes of the slice: x: 4, y: 4 (y_hi: 2, y_lo: 2; y = y_hi * 2 + y_lo), z: 8, core: 2. Of those that a mesh axis runs over, the one named last changes fastest.
Arguments:
- direction_nodal: float32 [1, 128, 2, 8192], P(None, 'tm', None, 'net'), may hold values from -27 to 27
- direction_capacity: float32 [1, 128, 65536], P(None, 'tm', 'net'), may hold values from -27 to 27
- residual_nodal: float32 [1, 128, 2, 8192], P(None, 'tm', None, 'net'), may hold values from -27 to 27
- residual_capacity: float32 [1, 128, 65536], P(None, 'tm', 'net'), may hold values from -27 to 27
- scale_flow: float32 [128, 12288], P('tm', 'net'), may hold values from 0.25 to 4
- scale_dispatch: float32 [128, 65536], P('tm', 'net'), may hold values from 0.25 to 4
- scale_storage: float32 [128, 2, 8192], P('tm', None, 'net'), may hold values from 0.25 to 4
- scale_capacity: float32 [65536], P('net'), may hold values from 0.02 to 0.3
- availability: float32 [128, 65536], P('tm', 'net'), may hold values from 0.05 to 1
- retention: float32 [8192], P('net'), may hold values from 0.5 to 1
- line_anchor: int32 [96], P('net'), may hold values from 0 to 63
- line_target: int32 [96], P('net'), may hold values from 0 to 63
- anchor_rows: int32 [12288], P('net'), may hold values from 0 to 127
- target_rows: int32 [12288], P('net'), may hold values from 0 to 127
- column_block: int32 [512], P('net'), may hold values from 0 to 63
- column_rows: int32 [65536], P('net'), may hold values from 0 to 127
Outputs:
- updated_nodal: float32 [1, 128, 2, 8192], P(None, 'tm', None, 'net')
- updated_capacity: float32 [1, 128, 65536], P(None, 'tm', 'net')
All inputs are finite; a program needn't handle non-finite values.
Results may differ from a plain program's by a relative error of at most 0.00002.
Values sent between devices are 32-bit elements; how exact they have to be, the bound alone decides.
No kernel may reach another device: no remote copies, remote signals or barrier semaphores. Data moves between devices by JAX's collectives and lax.ppermute only.
A program may use at most 64 MiB of HBM per device.

v0:
```python
import jax
import jax.numpy as jnp
from jax import lax
from jax.sharding import PartitionSpec as P

BLOCK = 128
DAMPING = 0.5


def passed_along(value, axis, steps):
    count = lax.axis_size(axis)
    pairs = [(source, (source + steps) % count) for source in range(count)]
    return lax.ppermute(value, axis, pairs)


def body(
    direction_nodal,
    direction_capacity,
    residual_nodal,
    residual_capacity,
    scale_flow,
    scale_dispatch,
    scale_storage,
    scale_capacity,
    availability,
    retention,
    line_anchor,
    line_target,
    anchor_rows,
    target_rows,
    column_block,
    column_rows,
):
    anchor = jnp.repeat(line_anchor, BLOCK) * BLOCK + anchor_rows
    target = jnp.repeat(line_target, BLOCK) * BLOCK + target_rows
    column_bus = jnp.repeat(column_block, BLOCK) * BLOCK + column_rows
    balance = direction_nodal[:, :, 0, :]
    storage = direction_nodal[:, :, 1, :]
    network = lax.all_gather(balance, "net", axis=2, tiled=True)
    next_first = passed_along(storage, "tm", -1)
    storage_next = jnp.concatenate([storage[:, 1:, :], next_first], axis=1)
    flow_value = jnp.take(network, anchor, axis=2) - jnp.take(network, target, axis=2)
    dispatch_value = jnp.take(network, column_bus, axis=2) + direction_capacity
    partial_sums = -jnp.sum(availability[None] * direction_capacity, axis=1)
    level_value = storage - retention * storage_next
    charge_value = balance - storage
    flow_scaled = scale_flow[None] * flow_value
    dispatch_scaled = scale_dispatch[None] * dispatch_value
    level_scaled = scale_storage[None, :, 0, :] * level_value
    charge_scaled = scale_storage[None, :, 1, :] * charge_value
    capacity_value = lax.psum(partial_sums, "tm")
    capacity_scaled = scale_capacity[None] * capacity_value
    squares_local = jnp.sum(residual_nodal * residual_nodal, axis=(1, 2, 3)) + jnp.sum(
        residual_capacity * residual_capacity, axis=(1, 2)
    )
    bus_terms = jnp.zeros(network.shape, jnp.float32).at[:, :, anchor].add(flow_scaled)
    bus_terms = (
        bus_terms.at[:, :, target].add(-flow_scaled).at[:, :, column_bus].add(dispatch_scaled)
    )
    own_terms = lax.psum_scatter(bus_terms, "net", scatter_dimension=2, tiled=True)
    image_balance = own_terms + charge_scaled + DAMPING * balance
    behind = passed_along(level_scaled, "tm", 1)
    level_before = jnp.concatenate([behind, level_scaled[:, :-1, :]], axis=1)
    image_storage = level_scaled - retention * level_before - charge_scaled + DAMPING * storage
    image_limit = (
        dispatch_scaled
        - availability[None] * capacity_scaled[:, None, :]
        + DAMPING * direction_capacity
    )
    image_nodal = jnp.stack([image_balance, image_storage], axis=2)
    curvature_local = jnp.sum(direction_nodal * image_nodal, axis=(1, 2, 3)) + jnp.sum(
        direction_capacity * image_limit, axis=(1, 2)
    )
    squares, curvature = lax.psum((squares_local, curvature_local), ("tm", "net"))
    step_size = squares / curvature
    updated_nodal = residual_nodal - step_size[:, None, None, None] * image_nodal
    updated_capacity = residual_capacity - step_size[:, None, None] * image_limit
    return (updated_nodal, updated_capacity)


def solution(mesh):
    in_specs = (
        P(None, "tm", None, "net"),
        P(None, "tm", "net"),
        P(None, "tm", None, "net"),
        P(None, "tm", "net"),
        P("tm", "net"),
        P("tm", "net"),
        P("tm", None, "net"),
        P("net"),
        P("tm", "net"),
        P("net"),
        P("net"),
        P("net"),
        P("net"),
        P("net"),
        P("net"),
        P("net"),
    )
    out_specs = (P(None, "tm", None, "net"), P(None, "tm", "net"))
    return jax.shard_map(body, mesh=mesh, in_specs=in_specs, out_specs=out_specs, check_vma=False)
```

profile of v0, /device:TPU:1, one launch (start us, length us, event | category | flops | bytes accessed | tf_op | source)
XLA Modules:
  0.0 1337.2 jit_solution(10901547301141026485)
XLA Ops:
  7.2 0.0 all-reduce.3.cloned.1.call-start
  7.2 1.8 fusion.3
  9.0 0.0 all-reduce.3.cloned.1.call-update
  9.0 0.0 reduce-scatter.4.cloned.1.call-start
  9.1 0.9 fusion.11
  9.9 3.3 collective-permute-start
  13.3 4.8 all-gather
  18.0 0.7 broadcast_multiply_fusion.1
  18.7 0.7 broadcast_multiply_fusion.2
  19.3 0.8 broadcast_clamp_fusion.1
  20.2 0.0 copy-start.10
  20.2 34.3 %gather_fusion.2 = f32[6144]{0:T(1024)S(1)} fusion(f32[8192]{0:T(1024)S(1)} %bitcast.85, s32[6144]{0:T(1024)S(1)} %get-tuple-element.12), kind=kCustom, calls=%fused_computation.1.clone | custom fusion | bytes 73728 | tf_op jit(solution)/shard_map/jit(_take)/gather | solution.py:42
  54.5 0.0 copy-done.10
  54.5 0.1 broadcast_clamp_fusion.2
  54.6 0.0 copy-start.12
  54.6 0.0 copy-start.4
  54.6 34.3 %gather_fusion.1 = f32[6144]{0:T(1024)S(1)} fusion(f32[8192]{0:T(1024)S(1)} %bitcast.86, s32[6144]{0:T(1024)S(1)} %get-tuple-element.14), kind=kCustom, calls=%fused_computation.clone | custom fusion | bytes 73728 | tf_op jit(solution)/shard_map/jit(_take)/gather | solution.py:42
  88.9 0.0 copy-done.12
  88.9 0.0 copy-done.4
  88.9 0.1 broadcast_clamp_fusion
  89.0 0.0 copy-start.11
  89.0 0.0 copy-start
  89.0 180.5 %gather_fusion = f32[32768]{0:T(1024)S(1)} fusion(f32[8192]{0:T(1024)S(1)} %bitcast.87, s32[32768]{0:T(1024)S(1)} %get-tuple-element.8), kind=kCustom, calls=%fused_computation.2 | custom fusion | bytes 393216 | tf_op jit(solution)/shard_map/jit(_take)/gather | solution.py:43
  269.6 0.0 copy-done.11
  269.7 0.1 fusion.10
  269.7 0.0 copy-done
  269.7 0.9 multiply_reduce_fusion.1
  270.6 42.8 %scatter_custom_fusion = f32[8192]{0:T(1024)S(1)} fusion(s32[6144]{0:T(1024)S(1)} %get-tuple-element.15, f32[6144]{0:T(1024)S(1)} %bitcast.99, f32[]{:T(128)} %constant.15.clone.1), kind=kCustom, calls=%fused_computation.36 | custom fusion | flops 6144 | bytes 32772 | tf_op jit(solution)/shard_map/scatter-add | solution.py:56
  313.4 0.0 copy-start.3
  313.5 0.0 copy-start.8
  313.5 0.0 copy-start.9
  313.5 0.0 copy-start.1
  313.5 0.0 copy-start.2
  313.5 0.0 copy-start.6
  313.5 0.0 copy-start.7
  313.5 42.9 %scatter_fusion = f32[8192]{0:T(1024)S(1)} fusion(f32[8192]{0:T(1024)S(1)} %scatter_custom_fusion, s32[6144]{0:T(1024)S(1)} %get-tuple-element.13, f32[6144]{0:T(1024)S(1)} %bitcast.94), kind=kCustom, calls=%fused_computation.4 | custom fusion | flops 6144 | bytes 98304 | tf_op jit(solution)/shard_map/scatter-add | solution.py:58
  356.4 0.0 collective-permute-done
  356.4 0.0 copy-done.3
  356.5 0.0 copy-done.8
  356.5 0.0 copy-done.9
  356.5 0.6 collective-permute-start.1
  357.1 593.0 %all-reduce.3.cloned.1.call-done = f32[1,32768]{1,0:T(1,128)} async-done(((f32[1,32768]{1,0:T(1,128)}), f32[1,32768]{1,0:T(1,128)}) %all-reduce.3.cloned.1.call-update) | async-done | bytes 131088 | tf_op jit(solution)/shard_map/psum | solution.py:51
  950.2 0.0 copy-done.1
  950.2 0.0 copy-done.2
  950.2 0.0 copy-done.6
  950.2 0.0 copy-done.7
  950.2 1.9 multiply_reduce_fusion
  952.1 225.9 %scatter_fusion.1 = f32[8192]{0:T(1024)S(1)} fusion(f32[8192]{0:T(1024)S(1)} %scatter_fusion, s32[32768]{0:T(1024)S(1)} %get-tuple-element.9, f32[32768]{0:T(1024)S(1)} %bitcast.91), kind=kCustom, calls=%fused_computation.5 | custom fusion | flops 32768 | bytes 524288 | tf_op jit(solution)/shard_map/scatter-add | solution.py:58
  1178.1 0.0 copy-start.5
  1178.1 6.4 copy.18
  1184.4 0.0 reduce-scatter.4.cloned.1.call-update
  1184.5 0.0 copy-done.5
  1184.5 0.6 multiply_reduce_fusion.3
  1186.3 57.5 %reduce-scatter.4.cloned.1.call-done = f32[4096,1]{1,0:T(8,128)} async-done(((f32[8192,1]{1,0:T(8,128)}), f32[4096,1]{1,0:T(8,128)}) %reduce-scatter.4.cloned.1.call-update) | async-done | bytes 16400
  1243.8 4.4 copy.19
  1248.3 0.0 collective-permute-done.1
  1248.3 0.1 fusion.5
  1248.4 0.7 multiply_reduce_fusion.2
  1250.4 77.2 %all-reduce = (f32[1]{0:T(128)}, f32[1]{0:T(128)}) all-reduce(f32[1]{0:T(128)} %bitcast.2, f32[1]{0:T(128)} %bitcast.31), channel_id=1, replica_groups=mesh['tm'=128,'net'=2] {'tm','net'}, use_global_device_ids=true, to_apply=%region_2.3 | all-reduce | flops 2 | bytes 16 | tf_op jit(solution)/shard_map/psum | solution.py:74
  1328.9 0.7 multiply_subtract_fusion.1
  1329.6 0.8 multiply_subtract_fusion
  (5 shorter events, 0.1 us)
Async XLA Ops:
  7.2 943.0 %all-reduce.3.cloned.1.call-start = ((), (), s32[]{:S(2)}) async-start(), calls=%async_computation.1 | async-start | bytes 262144 | tf_op jit(solution)/shard_map/psum | solution.py:51
  9.0 1234.8 %reduce-scatter.4.cloned.1.call-start = ((), (), s32[]{:S(2)}) async-start(), calls=%async_computation.2 | async-start | bytes 6291456
  9.9 346.5 %collective-permute-start = (f32[1,1,4096]{2,1,0:T(1,128)S(1)}, f32[1,1,4096]{2,1,0:T(1,128)S(1)}, u32[]{:S(2)}, u32[]{:S(2)}) collective-permute-start(f32[1,1,4096]{2,1,0:T(1,128)S(1)} %get-tuple-element.19), channel_id=1, source_target_pairs={{0,254},{2,0},{4,2},{6,4},{8,6},{10,8},{12,10},{14,12},{16,14},{18... | collective-permute-start | bytes 49160 | tf_op jit(solution)/shard_map/ppermute | solution.py:13
  20.2 34.3 %copy-start.10 = (s32[6144]{0:T(1024)S(1)}, s32[6144]{0:T(1024)}, u32[]{:S(2)}) copy-start(s32[6144]{0:T(1024)} %param.30) | copy-start | bytes 73732
  54.6 34.3 %copy-start.12 = (s32[256]{0:T(256)S(1)}, s32[256]{0:T(256)}, u32[]{:S(2)}) copy-start(s32[256]{0:T(256)} %param.32) | copy-start | bytes 3076
  54.6 34.3 %copy-start.4 = (s32[32768]{0:T(1024)S(1)}, s32[32768]{0:T(1024)}, u32[]{:S(2)}) copy-start(s32[32768]{0:T(1024)} %param.33) | copy-start | bytes 393220
  89.0 180.6 %copy-start.11 = (f32[1,6144]{1,0:T(1,128)S(1)}, f32[1,6144]{1,0:T(1,128)}, u32[]{:S(2)}) copy-start(f32[1,6144]{1,0:T(1,128)} %param.22) | copy-start | bytes 73732
  89.0 180.7 %copy-start = (f32[1,1,32768]{2,1,0:T(1,128)S(1)}, f32[1,1,32768]{2,1,0:T(1,128)}, u32[]{:S(2)}) copy-start(f32[1,1,32768]{2,1,0:T(1,128)} %param.21) | copy-start | bytes 393220
  313.4 43.0 %copy-start.3 = (f32[1,1,2,4096]{3,2,1,0:T(2,128)S(1)}, f32[1,1,2,4096]{3,2,1,0:T(2,128)}, u32[]{:S(2)}) copy-start(f32[1,1,2,4096]{3,2,1,0:T(2,128)} %param.18) | copy-start | bytes 98308
  313.5 43.0 %copy-start.8 = (f32[4096]{0:T(1024)S(1)}, f32[4096]{0:T(1024)}, u32[]{:S(2)}) copy-start(f32[4096]{0:T(1024)} %param.27) | copy-start | bytes 49156
  313.5 43.0 %copy-start.9 = (f32[1,2,4096]{2,1,0:T(2,128)S(1)}, f32[1,2,4096]{2,1,0:T(2,128)}, u32[]{:S(2)}) copy-start(f32[1,2,4096]{2,1,0:T(2,128)} %param.24) | copy-start | bytes 98308
  313.5 636.7 %copy-start.1 = (f32[1,1,32768]{2,1,0:T(1,128)S(1)}, f32[1,1,32768]{2,1,0:T(1,128)}, u32[]{:S(2)}) copy-start(f32[1,1,32768]{2,1,0:T(1,128)} %param.19) | copy-start | bytes 393220
  313.5 636.7 %copy-start.2 = (f32[1,32768]{1,0:T(1,128)S(1)}, f32[1,32768]{1,0:T(1,128)}, u32[]{:S(2)}) copy-start(f32[1,32768]{1,0:T(1,128)} %param.26) | copy-start | bytes 393220
  313.5 636.7 %copy-start.6 = (f32[32768]{0:T(1024)S(1)}, f32[32768]{0:T(1024)}, u32[]{:S(2)}) copy-start(f32[32768]{0:T(1024)} %param.25) | copy-start | bytes 393220
  313.5 636.7 %copy-start.7 = (f32[1,32768]{1,0:T(1,128)S(1)}, f32[1,32768]{1,0:T(1,128)}, u32[]{:S(2)}) copy-start(f32[1,32768]{1,0:T(1,128)} %param.23) | copy-start | bytes 393220
  356.5 891.7 %collective-permute-start.1 = (f32[1,1,4096]{2,1,0:T(1,128)S(1)}, f32[1,1,4096]{2,1,0:T(1,128)S(1)}, u32[]{:S(2)}, u32[]{:S(2)}) collective-permute-start(f32[1,1,4096]{2,1,0:T(1,128)S(1)} %subtract_multiply_fusion), channel_id=1, source_target_pairs={{0,2},{2,4},{4,6},{6,8},{8,10},{10,12},{12,14},{14,16},{16,18},{18... | collective-permute-start | bytes 49160 | tf_op jit(solution)/shard_map/ppermute | solution.py:13
  1178.1 6.4 copy-start.5
Sparse Core Ops, SparseCore 0:
  11.2 938.9 all-reduce.2
  1184.6 59.2 reduce-scatter.3
where the time goes:
time: 1340 us
  waiting for transfers between devices  651 us (49%)
  other arithmetic  322 us (24%)
  local copies, waits for them, and re-layouts  261 us (19%)
  blocking collectives  81.9 us (6%)
  between operations  18.3 us (1%)
    psum x1, waiting for transfers between devices, body(): capacity_value = lax.psum(partial_sums, 'tm')  593 us
    scatter-add x2, other arithmetic, body(): bus_terms.at[:, :, target].add(-flow_scaled).at[:, :, column_bus]  269 us
    gather x1, local copies, waits for them, and re-layouts, body(): dispatch_value = jnp.take(network, column_bus, axis=2) + direction_capacity  181 us
    psum x1, blocking collectives, body(): lax.psum((squares_local, curvature_local), ('tm', 'net'))  77.2 us
    unnamed x3, waiting for transfers between devices  57.5 us
    scatter-add x1, other arithmetic, body(): jnp.zeros(network.shape, jnp.float32).at[:, :, anchor].add(flow_scaled)  42.8 us
    gather x1, local copies, waits for them, and re-layouts, body(): jnp.take(network, target, axis=2)  34.3 us
    gather x1, local copies, waits for them, and re-layouts, body(): jnp.take(network, anchor, axis=2) - jnp.take(network, target, axis=2)  34.3 us
  transfers between devices with their start and end apart: 4, of which 2 were waited for; matrix products, arithmetic and copies ran while one was open for 43% of the time, Pallas kernels for 0%

commit v1 on v0

--- a/solution.py
+++ b/solution.py
@@ -71,7 +71,7 @@
     curvature_local = jnp.sum(direction_nodal * image_nodal, axis=(1, 2, 3)) + jnp.sum(
         direction_capacity * image_limit, axis=(1, 2)
     )
-    squares, curvature = lax.psum((squares_local, curvature_local), ("tm", "net"))
+    squares, curvature = lax.psum(lax.psum((squares_local, curvature_local), "net"), "tm")
     step_size = squares / curvature
     updated_nodal = residual_nodal - step_size[:, None, None, None] * image_nodal
     updated_capacity = residual_capacity - step_size[:, None, None] * image_limit

time: 1340 us -> 1550 us (1.16)
  blocking collectives: 81.9 us -> 289 us
    psum x1 -> x2, blocking collectives: 77.2 us -> 284 us  [the longest x1 277 us: body(): lax.psum(lax.psum((squares_local, curvature_local), 'net'), 'tm')]
  transfers between devices with their start and end apart: 4 -> 4, of which waited for: 2 -> 2; matrix products, arithmetic and copies ran while one was open for 43% -> 37% of each run, Pallas kernels for 0% -> 0%
where the time goes in v1:
time: 1550 us; the launch traced here: 1540 us
  waiting for transfers between devices  651 us (42%)
  other arithmetic  322 us (21%)
  blocking collectives  289 us (19%)
  local copies, waits for them, and re-layouts  261 us (17%)
  between operations  18.3 us (1%)
    psum x1, waiting for transfers between devices, body(): capacity_value = lax.psum(partial_sums, 'tm')  593 us
    psum x1, blocking collectives, body(): lax.psum(lax.psum((squares_local, curvature_local), 'net'), 'tm')  277 us
    scatter-add x2, other arithmetic, body(): bus_terms.at[:, :, target].add(-flow_scaled).at[:, :, column_bus]  269 us
    gather x1, local copies, waits for them, and re-layouts, body(): dispatch_value = jnp.take(network, column_bus, axis=2) + direction_capacity  181 us
    unnamed x3, waiting for transfers between devices  57.5 us
    scatter-add x1, other arithmetic, body(): jnp.zeros(network.shape, jnp.float32).at[:, :, anchor].add(flow_scaled)  42.8 us
    gather x1, local copies, waits for them, and re-layouts, body(): jnp.take(network, target, axis=2)  34.3 us
    gather x1, local copies, waits for them, and re-layouts, body(): jnp.take(network, anchor, axis=2) - jnp.take(network, target, axis=2)  34.3 us
  transfers between devices with their start and end apart: 4, of which 2 were waited for; matrix products, arithmetic and copies ran while one was open for 37% of the time, Pallas kernels for 0%

profile of v1, /device:TPU:1, one launch (start us, length us, event | category | flops | bytes accessed | tf_op | source)
XLA Modules:
  0.0 1544.3 jit_solution(13685873771488752104)
XLA Ops:
  7.2 0.0 all-reduce.4.cloned.1.call-start
  7.2 1.8 fusion.3
  9.0 0.0 all-reduce.4.cloned.1.call-update
  9.0 0.0 reduce-scatter.4.cloned.1.call-start
  9.1 0.9 fusion.11
  9.9 3.3 collective-permute-start
  13.3 4.8 all-gather
  18.0 0.7 broadcast_multiply_fusion.1
  18.7 0.7 broadcast_multiply_fusion.2
  19.3 0.8 broadcast_clamp_fusion.1
  20.2 0.0 copy-start.10
  20.2 34.3 %gather_fusion.2 = f32[6144]{0:T(1024)S(1)} fusion(f32[8192]{0:T(1024)S(1)} %bitcast.85, s32[6144]{0:T(1024)S(1)} %get-tuple-element.14), kind=kCustom, calls=%fused_computation.1.clone | custom fusion | bytes 73728 | tf_op jit(solution)/shard_map/jit(_take)/gather | solution.py:42
  54.5 0.0 copy-done.10
  54.5 0.1 broadcast_clamp_fusion.2
  54.6 0.0 copy-start.12
  54.6 0.0 copy-start.4
  54.6 34.3 %gather_fusion.1 = f32[6144]{0:T(1024)S(1)} fusion(f32[8192]{0:T(1024)S(1)} %bitcast.86, s32[6144]{0:T(1024)S(1)} %get-tuple-element.16), kind=kCustom, calls=%fused_computation.clone | custom fusion | bytes 73728 | tf_op jit(solution)/shard_map/jit(_take)/gather | solution.py:42
  88.9 0.0 copy-done.12
  88.9 0.0 copy-done.4
  88.9 0.1 broadcast_clamp_fusion
  89.0 0.0 copy-start.11
  89.0 0.0 copy-start
  89.0 180.5 %gather_fusion = f32[32768]{0:T(1024)S(1)} fusion(f32[8192]{0:T(1024)S(1)} %bitcast.87, s32[32768]{0:T(1024)S(1)} %get-tuple-element.10), kind=kCustom, calls=%fused_computation.2 | custom fusion | bytes 393216 | tf_op jit(solution)/shard_map/jit(_take)/gather | solution.py:43
  269.6 0.0 copy-done.11
  269.7 0.1 fusion.10
  269.7 0.0 copy-done
  269.7 0.9 multiply_reduce_fusion.1
  270.6 42.8 %scatter_custom_fusion = f32[8192]{0:T(1024)S(1)} fusion(s32[6144]{0:T(1024)S(1)} %get-tuple-element.17, f32[6144]{0:T(1024)S(1)} %bitcast.99, f32[]{:T(128)} %constant.15.clone.1), kind=kCustom, calls=%fused_computation.36 | custom fusion | flops 6144 | bytes 32772 | tf_op jit(solution)/shard_map/scatter-add | solution.py:56
  313.4 0.0 copy-start.3
  313.5 0.0 copy-start.8
  313.5 0.0 copy-start.9
  313.5 0.0 copy-start.1
  313.5 0.0 copy-start.2
  313.5 0.0 copy-start.6
  313.5 0.0 copy-start.7
  313.5 42.9 %scatter_fusion = f32[8192]{0:T(1024)S(1)} fusion(f32[8192]{0:T(1024)S(1)} %scatter_custom_fusion, s32[6144]{0:T(1024)S(1)} %get-tuple-element.15, f32[6144]{0:T(1024)S(1)} %bitcast.94), kind=kCustom, calls=%fused_computation.4 | custom fusion | flops 6144 | bytes 98304 | tf_op jit(solution)/shard_map/scatter-add | solution.py:58
  356.4 0.0 collective-permute-done
  356.4 0.0 copy-done.3
  356.5 0.0 copy-done.8
  356.5 0.0 copy-done.9
  356.5 0.6 collective-permute-start.1
  357.1 593.0 %all-reduce.4.cloned.1.call-done = f32[1,32768]{1,0:T(1,128)} async-done(((f32[1,32768]{1,0:T(1,128)}), f32[1,32768]{1,0:T(1,128)}) %all-reduce.4.cloned.1.call-update) | async-done | bytes 131088 | tf_op jit(solution)/shard_map/psum | solution.py:51
  950.2 0.0 copy-done.1
  950.2 0.0 copy-done.2
  950.2 0.0 copy-done.6
  950.2 0.0 copy-done.7
  950.2 1.9 multiply_reduce_fusion
  952.1 225.9 %scatter_fusion.1 = f32[8192]{0:T(1024)S(1)} fusion(f32[8192]{0:T(1024)S(1)} %scatter_fusion, s32[32768]{0:T(1024)S(1)} %get-tuple-element.11, f32[32768]{0:T(1024)S(1)} %bitcast.91), kind=kCustom, calls=%fused_computation.5 | custom fusion | flops 32768 | bytes 524288 | tf_op jit(solution)/shard_map/scatter-add | solution.py:58
  1178.1 0.0 copy-start.5
  1178.1 6.4 copy.18
  1184.4 0.0 reduce-scatter.4.cloned.1.call-update
  1184.5 0.0 copy-done.5
  1184.5 0.6 multiply_reduce_fusion.3
  1186.3 57.5 %reduce-scatter.4.cloned.1.call-done = f32[4096,1]{1,0:T(8,128)} async-done(((f32[8192,1]{1,0:T(8,128)}), f32[4096,1]{1,0:T(8,128)}) %reduce-scatter.4.cloned.1.call-update) | async-done | bytes 16400
  1243.8 4.4 copy.19
  1248.3 0.0 collective-permute-done.1
  1248.3 0.1 fusion.5
  1248.4 0.7 multiply_reduce_fusion.2
  1250.4 6.9 all-reduce.1
  1257.3 277.4 %all-reduce = (f32[1]{0:T(128)}, f32[1]{0:T(128)}) all-reduce(f32[1]{0:T(128)} %get-tuple-element.5, f32[1]{0:T(128)} %get-tuple-element.6), channel_id=1, replica_groups=mesh['tm'=128,'net'=2] {'tm'}, use_global_device_ids=true, to_apply=%region_3.4 | all-reduce | flops 2 | bytes 16 | tf_op jit(solution)/shard_map/psum | solution.py:74
  1536.0 0.7 multiply_subtract_fusion.1
  1536.7 0.8 multiply_subtract_fusion
  (5 shorter events, 0.1 us)
Async XLA Ops:
  7.2 943.0 %all-reduce.4.cloned.1.call-start = ((), (), s32[]{:S(2)}) async-start(), calls=%async_computation.1 | async-start | bytes 262144 | tf_op jit(solution)/shard_map/psum | solution.py:51
  9.0 1234.8 %reduce-scatter.4.cloned.1.call-start = ((), (), s32[]{:S(2)}) async-start(), calls=%async_computation.2 | async-start | bytes 6291456
  9.9 346.5 %collective-permute-start = (f32[1,1,4096]{2,1,0:T(1,128)S(1)}, f32[1,1,4096]{2,1,0:T(1,128)S(1)}, u32[]{:S(2)}, u32[]{:S(2)}) collective-permute-start(f32[1,1,4096]{2,1,0:T(1,128)S(1)} %get-tuple-element.21), channel_id=1, source_target_pairs={{0,254},{2,0},{4,2},{6,4},{8,6},{10,8},{12,10},{14,12},{16,14},{18... | collective-permute-start | bytes 49160 | tf_op jit(solution)/shard_map/ppermute | solution.py:13
  20.2 34.3 %copy-start.10 = (s32[6144]{0:T(1024)S(1)}, s32[6144]{0:T(1024)}, u32[]{:S(2)}) copy-start(s32[6144]{0:T(1024)} %param.30) | copy-start | bytes 73732
  54.6 34.3 %copy-start.12 = (s32[256]{0:T(256)S(1)}, s32[256]{0:T(256)}, u32[]{:S(2)}) copy-start(s32[256]{0:T(256)} %param.32) | copy-start | bytes 3076
  54.6 34.3 %copy-start.4 = (s32[32768]{0:T(1024)S(1)}, s32[32768]{0:T(1024)}, u32[]{:S(2)}) copy-start(s32[32768]{0:T(1024)} %param.33) | copy-start | bytes 393220
  89.0 180.6 %copy-start.11 = (f32[1,6144]{1,0:T(1,128)S(1)}, f32[1,6144]{1,0:T(1,128)}, u32[]{:S(2)}) copy-start(f32[1,6144]{1,0:T(1,128)} %param.22) | copy-start | bytes 73732
  89.0 180.7 %copy-start = (f32[1,1,32768]{2,1,0:T(1,128)S(1)}, f32[1,1,32768]{2,1,0:T(1,128)}, u32[]{:S(2)}) copy-start(f32[1,1,32768]{2,1,0:T(1,128)} %param.21) | copy-start | bytes 393220
  313.4 43.0 %copy-start.3 = (f32[1,1,2,4096]{3,2,1,0:T(2,128)S(1)}, f32[1,1,2,4096]{3,2,1,0:T(2,128)}, u32[]{:S(2)}) copy-start(f32[1,1,2,4096]{3,2,1,0:T(2,128)} %param.18) | copy-start | bytes 98308
  313.5 43.0 %copy-start.8 = (f32[4096]{0:T(1024)S(1)}, f32[4096]{0:T(1024)}, u32[]{:S(2)}) copy-start(f32[4096]{0:T(1024)} %param.27) | copy-start | bytes 49156
  313.5 43.0 %copy-start.9 = (f32[1,2,4096]{2,1,0:T(2,128)S(1)}, f32[1,2,4096]{2,1,0:T(2,128)}, u32[]{:S(2)}) copy-start(f32[1,2,4096]{2,1,0:T(2,128)} %param.24) | copy-start | bytes 98308
  313.5 636.7 %copy-start.1 = (f32[1,1,32768]{2,1,0:T(1,128)S(1)}, f32[1,1,32768]{2,1,0:T(1,128)}, u32[]{:S(2)}) copy-start(f32[1,1,32768]{2,1,0:T(1,128)} %param.19) | copy-start | bytes 393220
  313.5 636.7 %copy-start.2 = (f32[1,32768]{1,0:T(1,128)S(1)}, f32[1,32768]{1,0:T(1,128)}, u32[]{:S(2)}) copy-start(f32[1,32768]{1,0:T(1,128)} %param.26) | copy-start | bytes 393220
  313.5 636.7 %copy-start.6 = (f32[32768]{0:T(1024)S(1)}, f32[32768]{0:T(1024)}, u32[]{:S(2)}) copy-start(f32[32768]{0:T(1024)} %param.25) | copy-start | bytes 393220
  313.5 636.7 %copy-start.7 = (f32[1,32768]{1,0:T(1,128)S(1)}, f32[1,32768]{1,0:T(1,128)}, u32[]{:S(2)}) copy-start(f32[1,32768]{1,0:T(1,128)} %param.23) | copy-start | bytes 393220
  356.5 891.7 %collective-permute-start.1 = (f32[1,1,4096]{2,1,0:T(1,128)S(1)}, f32[1,1,4096]{2,1,0:T(1,128)S(1)}, u32[]{:S(2)}, u32[]{:S(2)}) collective-permute-start(f32[1,1,4096]{2,1,0:T(1,128)S(1)} %subtract_multiply_fusion), channel_id=1, source_target_pairs={{0,2},{2,4},{4,6},{6,8},{8,10},{10,12},{12,14},{14,16},{16,18},{18... | collective-permute-start | bytes 49160 | tf_op jit(solution)/shard_map/ppermute | solution.py:13
  1178.1 6.4 copy-start.5
Sparse Core Ops, SparseCore 0:
  11.2 938.9 all-reduce.3
  1184.6 59.2 reduce-scatter.3
